TPU v7x, 256 devices: a whole 4x4x8 slice. The times are simulated.
256 devices in a mesh: row: 32 (over x, y, core), col: 8 (over z).
Axes of the slice: x: 4, y: 4, z: 8, core: 2. Of those that a mesh axis runs over, the one named last changes fastest.
Arguments:
- features: bfloat16 [8192, 1024], P('row', 'col'), may hold values from -6 to 6
- grad_out: bfloat16 [8192, 1024], P('row', 'col'), may hold values from -6 to 6
- weight: bfloat16 [1024, 1024], replicated, may hold values from -0.1875 to 0.1875
- root_weight: bfloat16 [1024, 1024], replicated, may hold values from -0.1875 to 0.1875
- values: bfloat16 [32, 8, 8, 128, 128], P('row', 'col'), may hold values from -0.125 to 0.125
- positions: int32 [32, 8, 8], P('row', 'col'), may hold values from 0 to 15, as said below
- counts: int32 [32, 8], P('row', 'col'), may hold values from 1 to 8, as said below
Outputs:
- activations: bfloat16 [8192, 1024], P('row', 'col')
- feature_grad: float32 [8192, 1024], P('row', 'col')
- weight_grad: float32 [1024, 1024], P('col')
- root_grad: float32 [1024, 1024], P('col')
Inputs may be any that keep to these rules, and one draw needn't show every extreme that they name: Within the first counts slots of a tile the positions are distinct; position p is block row p // 8 and block column p % 8 of the tile. `counts`: some tile uses all 8 slots in every draw; about a quarter of the block rows have much fuller tiles (4 or 8 used slots) than the rest (1 or 2).
All inputs are finite; a program needn't handle non-finite values.
Results may differ from a plain program's by a relative error of at most 0.012.
Values may be sent and summed in bfloat16 or wider, within the bound.
No kernel may reach another device: no remote copies, remote signals or barrier semaphores. Data moves between devices by JAX's collectives and lax.ppermute only.
A program may use at most 64 MiB of HBM per device.

v0:
```python
import math
import jax
import jax.numpy as jnp
from jax import lax
from jax.sharding import PartitionSpec as P


def silu_grad(preact):
    sig = jax.nn.sigmoid(preact)
    return sig * (1.0 + preact * (1.0 - sig))


def gather_rows(block, axis_name, parts):
    spread = jnp.broadcast_to(block[None], (parts,) + block.shape)
    got = lax.all_to_all(spread, axis_name, 0, 0, tiled=True)
    return got.reshape((parts * block.shape[0],) + block.shape[1:])


def reduce_rows(block, axis_name, parts):
    pieces = block.reshape((parts, block.shape[0] // parts) + block.shape[1:])
    got = lax.all_to_all(pieces, axis_name, 0, 0, tiled=True)
    return got.astype(jnp.float32).sum(0)


def per_device(features, grad_out, weight, root_weight, values, positions, counts):
    node_rows, feat_dev = features.shape
    slots, block_edge = (values.shape[2], values.shape[-1])
    row_blocks = node_rows // block_edge
    col_count = lax.axis_size("col")
    row_count = lax.axis_size("row")
    col_index = lax.axis_index("col")
    live = (jnp.arange(slots, dtype=jnp.int32) < counts[0, 0]).astype(values.dtype)
    own_vals = (values[0, 0] * live[:, None, None]).reshape(slots * block_edge, block_edge)
    pos_row = jnp.zeros((block_edge, block_edge), values.dtype)
    pos_row = lax.dynamic_update_slice(
        pos_row, positions[0, 0].astype(values.dtype).reshape(1, slots), (0, 0)
    )
    packed = jnp.concatenate([own_vals, pos_row, features, grad_out], axis=0)
    all_packed = lax.all_gather(packed, "col", axis=0, tiled=True).reshape(
        col_count, packed.shape[0], block_edge
    )
    tile_vals = all_packed.reshape(col_count, -1, block_edge, block_edge)[:, :slots]
    tile_pos = all_packed[:, slots * block_edge, :slots].astype(jnp.int32)
    cb = row_count * node_rows // col_count // block_edge
    n_pos = row_blocks * cb
    onehot = (tile_pos[:, :, None] == jnp.arange(n_pos, dtype=jnp.int32)[None, None, :]).astype(
        values.dtype
    )
    dense = jnp.einsum(
        "tsp,tsij->tpij", onehot, tile_vals, preferred_element_type=jnp.float32
    ).astype(values.dtype)
    dense = dense.reshape(col_count, row_blocks, cb, block_edge, block_edge)
    x_all = gather_rows(features, "row", row_count)
    x_tiles = x_all.reshape(col_count, cb, block_edge, feat_dev)
    col_hot = (
        (tile_pos % cb)[:, :, None] == jnp.arange(cb, dtype=jnp.int32)[None, None, :]
    ).astype(values.dtype)
    row_hot = (
        (tile_pos // cb)[:, :, None] == jnp.arange(row_blocks, dtype=jnp.int32)[None, None, :]
    ).astype(jnp.float32)
    chosen = jnp.einsum(
        "tsc,tcjf->tsjf", col_hot, x_tiles, preferred_element_type=jnp.float32
    ).astype(values.dtype)
    products = jnp.einsum("tsij,tsjf->tsif", tile_vals, chosen, preferred_element_type=jnp.float32)
    agg_f32 = jnp.sum(products[:, :, None] * row_hot[:, :, :, None, None], axis=(0, 1))
    aggregated = agg_f32.reshape(node_rows, feat_dev).astype(jnp.bfloat16)
    agg_parts = gather_rows(aggregated, "col", col_count).reshape(col_count, node_rows, feat_dev)
    nodes = row_count * node_rows
    dense_t = jnp.transpose(dense, (0, 2, 4, 1, 3)).reshape(nodes, node_rows)
    agg_parts, dense_t = lax.optimization_barrier((agg_parts, dense_t))
    agg_full = jnp.moveaxis(agg_parts, 0, 1).reshape(node_rows, col_count * feat_dev)
    pair_parts = all_packed[:, (slots + 1) * block_edge :].reshape(
        col_count, 2, node_rows, feat_dev
    )
    pair_full = jnp.moveaxis(pair_parts, 0, 2).reshape(2, node_rows, col_count * feat_dev)
    feat_full = pair_full[0]
    grad_full = pair_full[1]
    preact = jnp.dot(agg_full, weight, preferred_element_type=jnp.float32) + jnp.dot(
        feat_full, root_weight, preferred_element_type=jnp.float32
    )
    preact_own = lax.dynamic_slice_in_dim(preact, col_index * feat_dev, feat_dev, 1)
    activations = jax.nn.silu(preact_own).astype(jnp.bfloat16)
    preact_grad = (grad_full.astype(jnp.float32) * silu_grad(preact)).astype(jnp.bfloat16)
    contract_rows = (((0,), (0,)), ((), ()))
    weight_part = lax.dot_general(
        aggregated, preact_grad, contract_rows, preferred_element_type=jnp.float32
    )
    root_part = lax.dot_general(
        features, preact_grad, contract_rows, preferred_element_type=jnp.float32
    )
    grad_scale = 1.0 / math.sqrt(nodes)
    both = jnp.concatenate([weight_part, root_part], axis=0) * grad_scale
    sum_rows = both.shape[0] // row_count
    lane_tiles = both.shape[1] // block_edge
    sum_lanes = sum_rows * lane_tiles
    both_tiled = (
        both.astype(jnp.bfloat16)
        .reshape(row_count, sum_rows, lane_tiles, block_edge)
        .transpose(0, 2, 1, 3)
        .reshape(row_count * sum_lanes, block_edge)
    )
    sum_pair = reduce_rows(both_tiled, "row", row_count).astype(jnp.bfloat16)
    w_rows = lax.dynamic_slice_in_dim(weight, col_index * feat_dev, feat_dev, 0)
    r_rows = lax.dynamic_slice_in_dim(root_weight, col_index * feat_dev, feat_dev, 0)
    contract_cols = (((1,), (1,)), ((), ()))
    aggregated_grad = lax.dot_general(
        preact_grad, w_rows, contract_cols, preferred_element_type=jnp.float32
    ).astype(jnp.bfloat16)
    own_grad = lax.dot_general(
        preact_grad, r_rows, contract_cols, preferred_element_type=jnp.float32
    )
    column_terms = jnp.dot(dense_t, aggregated_grad, preferred_element_type=jnp.float32)
    term_pieces = column_terms.astype(jnp.bfloat16).reshape(row_count, node_rows, feat_dev)
    room = jnp.zeros((row_count,) + sum_pair.shape, term_pieces.dtype)
    outgoing = jnp.concatenate([term_pieces, room], axis=1)
    outgoing, own_grad = lax.optimization_barrier((outgoing, own_grad))
    outgoing = lax.dynamic_update_slice(
        outgoing, jnp.broadcast_to(sum_pair[None], room.shape), (0, node_rows, 0)
    )
    incoming = lax.all_to_all(outgoing, "row", 0, 0, tiled=True)
    summed_cols = incoming[:, :node_rows].astype(jnp.float32).sum(0)
    got_sums = (
        incoming[:, node_rows:]
        .reshape(row_count, lane_tiles, sum_rows, block_edge)
        .transpose(0, 2, 1, 3)
        .astype(jnp.float32)
    )
    half = row_count // 2
    weight_sum = got_sums[:half].reshape(feat_dev, -1)
    root_sum = got_sums[half:].reshape(feat_dev, -1)
    feature_grad = summed_cols + own_grad
    return (activations, feature_grad, weight_sum, root_sum)


def solution(mesh):
    in_specs = (
        P("row", "col"),
        P("row", "col"),
        P(),
        P(),
        P("row", "col", None, None, None),
        P("row", "col", None),
        P("row", "col"),
    )
    out_specs = (P("row", "col"), P("row", "col"), P("col", None), P("col", None))
    return jax.shard_map(
        per_device, mesh=mesh, in_specs=in_specs, out_specs=out_specs, check_vma=False
    )
```

profile of v0, /device:TPU:1, one launch (start us, length us, event | category | flops | bytes accessed | tf_op | source)
XLA Modules:
  0.0 168.5 jit_solution(12683011915921730170)
XLA Ops:
  9.9 1.7 fusion.17
  11.6 2.6 %broadcast_in_dim.6 = bf16[32,256,128]{2,1,0:T(8,128)(2,1)} broadcast(bf16[256,128]{1,0:T(8,128)(2,1)} %param.7), dimensions={1,2} | broadcast | bytes 2162688 | tf_op jit(solution)/shard_map/broadcast_in_dim | solution.py:14
  14.2 8.6 %all-to-all-start = ((bf16[32,256,128]{2,1,0:T(8,128)(2,1)}), bf16[32,256,128]{2,1,0:T(8,128)(2,1)}, u32[]{:S(2)}, u32[]{:S(2)}) async-start(bf16[32,256,128]{2,1,0:T(8,128)(2,1)} %broadcast_in_dim.6), calls=%async_computation | async-start | bytes 4194304 | tf_op jit(solution)/shard_map/all_to_all | solution.py:15
  22.9 39.9 %all-gather.2.cloned.1.call-done = bf16[13312,128]{1,0:T(8,128)(2,1)} async-done(((bf16[1664,128]{1,0:T(8,128)(2,1)}), bf16[13312,128]{1,0:T(8,128)(2,1)}) %all-gather.2.cloned.1.call-update) | async-done | bytes 3407888 | tf_op jit(solution)/shard_map/all_gather | solution.py:39
  63.6 3.1 %fusion.5 = bf16[8,8,128,128]{3,1,2,0:T(8,128)(2,1)S(1)} fusion(bf16[8,8,128,128]{3,2,1,0:T(8,128)(2,1)} %bitcast.9, s32[8,8]{1,0:T(8,128)S(1)} %get-tuple-element.16), kind=kOutput, calls=%fused_computation.10 | convolution fusion | flops 17826304 | bytes 4194560 | tf_op jit(solution)/shard_map/tsc,tcjf->tsjf/dot_general | solution.py:61
  69.1 4.2 %all-to-all-start.1 = ((bf16[8,256,128]{1,2,0:T(8,128)(2,1)}), bf16[8,256,128]{1,2,0:T(8,128)(2,1)}, u32[]{:S(2)}, u32[]{:S(2)}) async-start(bf16[8,256,128]{1,2,0:T(8,128)(2,1)} %broadcast_in_dim.7), calls=%async_computation.1 | async-start | bytes 1048576 | tf_op jit(solution)/shard_map/all_to_all | solution.py:15
  73.2 1.3 slice.40
  74.6 1.8 %slice.39 = bf16[8,8,128,128]{3,2,1,0:T(8,128)(2,1)S(1)} slice(bf16[8,13,128,128]{3,2,1,0:T(8,128)(2,1)} %bitcast.89), slice={[0:8], [0:8], [0:128], [0:128]} | slice | bytes 4194304 | tf_op jit(solution)/shard_map/slice | solution.py:42
  77.1 1.9 %convert_bitcast_fusion = bf16[8,2,8,128,128]{4,2,1,3,0:T(8,128)(2,1)S(1)} fusion(bf16[8,8,128,128]{3,2,1,0:T(8,128)(2,1)S(1)} %slice.39, s32[8,8]{1,0:T(8,128)S(1)} %bitcast.96), kind=kOutput, calls=%fused_computation.4 | convolution fusion | flops 35652608 | bytes 6291712 | tf_op jit(solution)/shard_map/tsp,tsij->tpij/dot_general | solution.py:49
  79.0 3.2 %copy.47 = bf16[8,2,8,128,128]{4,2,0,3,1:T(8,128)(2,1)} copy(bf16[8,2,8,128,128]{4,2,1,3,0:T(8,128)(2,1)S(1)} %convert_bitcast_fusion) | data formatting | bytes 8388608 | tf_op jit(solution)/shard_map/reshape | solution.py:52
  82.1 7.3 %reshape.122 = bf16[8192,256]{0,1:T(8,128)(2,1)} reshape(bf16[8,8,128,2,128]{2,1,0,4,3:T(8,128)(2,1)} %bitcast.83) | data formatting | bytes 8388608 | tf_op jit(solution)/shard_map/reshape | solution.py:69
  89.4 1.2 slice_convert_fusion
  91.2 1.9 %fusion.34 = f32[256,1024]{1,0:T(8,128)S(1)} fusion(bf16[256,1024]{0,1:T(8,128)(2,1)} %bitcast.16, bf16[1024,1024]{1,0:T(8,128)(2,1)S(1)} %copy-done), kind=kOutput, calls=%fused_computation.62 | convolution fusion | flops 536870912 | bytes 3670016 | tf_op jit(solution)/shard_map/dot_general | solution.py:78
  93.4 2.1 %fusion.8 = (bf16[256,1024]{1,0:T(8,128)(2,1)S(1)}, f32[256,1024]{1,0:T(8,128)}) fusion(f32[32,8,8,128]{3,2,1,0:T(8,128)S(1)} %bitcast.91, f32[256,1024]{1,0:T(8,128)S(1)} %fusion.34, bf16[1024,1024]{1,0:T(8,128)(2,1)S(1)} %copy-done.5, bf16[32,8,8,128]{3,2,1,0:T(8,128)(2,1)S(1)} %bitcast.94), kind=kOutput, calls=%fused_computation.17 | convolution fusion | flops 539492352 | bytes 6291456 | tf_op jit(solution)/shard_map/dot_general | solution.py:78
  97.0 7.4 %all-to-all-start.2 = ((bf16[32,64,128]{2,1,0:T(8,128)(2,1)}), bf16[32,64,128]{2,1,0:T(8,128)(2,1)S(1)}, u32[]{:S(2)}, u32[]{:S(2)}) async-start(bf16[32,64,128]{2,1,0:T(8,128)(2,1)} %fusion.12), calls=%async_computation.2 | async-start | bytes 1048576 | tf_op jit(solution)/shard_map/all_to_all | solution.py:21
  104.3 5.3 %convolution_convert_fusion = bf16[8192,128]{1,0:T(8,128)(2,1)} fusion(bf16[8192,256]{0,1:T(8,128)(2,1)} %reshape.122, bf16[256,1024]{1,0:T(8,128)(2,1)S(1)} %get-tuple-element.18, bf16[1024,1024]{1,0:T(8,128)(2,1)S(1)} %copy-done, s32[]{:T(128)S(6)} %select_n.27), kind=kOutput, calls=%fused_computation | convolution fusion | flops 605061120 | bytes 7077892 | tf_op jit(solution)/shard_map/dot_general | solution.py:112
  109.7 3.5 %concatenate.10 = bf16[32,320,128]{2,1,0:T(8,128)(2,1)} pad(bf16[32,256,128]{2,1,0:T(8,128)(2,1)} %bitcast.84, bf16[]{:T(256)} %constant.37.clone.1), padding=0_0x0_64x0_0 | pad | bytes 4718594 | tf_op jit(solution)/shard_map/concatenate | solution.py:115
  113.1 1.2 fusion.18
  114.4 1.6 all-to-all-done.2
  117.0 5.9 %all-to-all-start.3 = ((bf16[32,320,128]{2,1,0:T(8,128)(2,1)}), bf16[32,320,128]{2,1,0:T(8,128)(2,1)}, u32[]{:S(2)}, u32[]{:S(2)}) async-start(bf16[32,320,128]{2,1,0:T(8,128)(2,1)} %broadcast_dynamic-update-slice_fusion), calls=%async_computation.3 | async-start | bytes 5242880 | tf_op jit(solution)/shard_map/all_to_all | solution.py:120
  122.9 1.6 multiply_convert_fusion
  124.5 32.4 %all-to-all-done.3 = bf16[32,320,128]{2,1,0:T(8,128)(2,1)} async-done(((bf16[32,320,128]{2,1,0:T(8,128)(2,1)}), bf16[32,320,128]{2,1,0:T(8,128)(2,1)}, u32[]{:S(2)}, u32[]{:S(2)}) %all-to-all-start.3) | async-done | bytes 2621472 | tf_op jit(solution)/shard_map/all_to_all | solution.py:120
  156.9 1.1 convert_bitcast_fusion.1
  159.1 1.9 %convert_reduce_fusion = f32[256,128]{1,0:T(8,128)S(1)} fusion(bf16[32,320,128]{2,1,0:T(8,128)(2,1)} %all-to-all-done.3), kind=kLoop, calls=%fused_computation.3 | loop fusion | flops 2064384 | bytes 2228224 | tf_op jit(solution)/shard_map/reduce_sum | solution.py:121
  (35 shorter events, 11.0 us)
Async XLA Ops:
  7.2 84.0 %copy-start = (bf16[1024,1024]{1,0:T(8,128)(2,1)S(1)}, bf16[1024,1024]{1,0:T(8,128)(2,1)}, u32[]{:S(2)}) copy-start(bf16[1024,1024]{1,0:T(8,128)(2,1)} %param.9) | copy-start | bytes 6291460
  7.2 55.6 %all-gather.2.cloned.1.call-start = ((), (), s32[]{:S(2)}) async-start(), calls=%async_computation.4 | async-start | bytes 3833856 | tf_op jit(solution)/shard_map/all_gather | solution.py:39
  14.2 49.3 %all-to-all-start = ((bf16[32,256,128]{2,1,0:T(8,128)(2,1)}), bf16[32,256,128]{2,1,0:T(8,128)(2,1)}, u32[]{:S(2)}, u32[]{:S(2)}) async-start(bf16[32,256,128]{2,1,0:T(8,128)(2,1)} %broadcast_in_dim.6), calls=%async_computation | async-start | bytes 4194304 | tf_op jit(solution)/shard_map/all_to_all | solution.py:15
  63.6 3.1 %copy-start.1 = (bf16[13312,128]{1,0:T(8,128)(2,1)S(1)}, bf16[13312,128]{1,0:T(8,128)(2,1)}, u32[]{:S(2)}) copy-start(bf16[13312,128]{1,0:T(8,128)(2,1)} %all-gather.2.cloned.1.call-done) | copy-start | bytes 10223620
  69.1 22.1 %all-to-all-start.1 = ((bf16[8,256,128]{1,2,0:T(8,128)(2,1)}), bf16[8,256,128]{1,2,0:T(8,128)(2,1)}, u32[]{:S(2)}, u32[]{:S(2)}) async-start(bf16[8,256,128]{1,2,0:T(8,128)(2,1)} %broadcast_in_dim.7), calls=%async_computation.1 | async-start | bytes 1048576 | tf_op jit(solution)/shard_map/all_to_all | solution.py:15
  91.2 1.9 %copy-start.2 = (f32[1,256,8,128]{3,2,1,0:T(8,128)S(1)}, f32[1,256,8,128]{3,2,1,0:T(8,128)}, u32[]{:S(2)}) copy-start(f32[1,256,8,128]{3,2,1,0:T(8,128)} %get-tuple-element.14) | copy-start | bytes 3145732
  91.2 1.9 %copy-start.4 = (bf16[1,256,8,128]{3,2,1,0:T(8,128)(2,1)S(1)}, bf16[1,256,8,128]{3,2,1,0:T(8,128)(2,1)}, u32[]{:S(2)}) copy-start(bf16[1,256,8,128]{3,2,1,0:T(8,128)(2,1)} %get-tuple-element.15) | copy-start | bytes 1572868
  91.2 2.2 %copy-start.5 = (bf16[1024,1024]{1,0:T(8,128)(2,1)S(1)}, bf16[1024,1024]{1,0:T(8,128)(2,1)}, u32[]{:S(2)}) copy-start(bf16[1024,1024]{1,0:T(8,128)(2,1)} %param.10) | copy-start | bytes 6291460
  93.4 2.1 %copy-start.3 = (bf16[256,128]{1,0:T(8,128)(2,1)S(1)}, bf16[256,128]{1,0:T(8,128)(2,1)}, u32[]{:S(2)}) copy-start(bf16[256,128]{1,0:T(8,128)(2,1)} %param.7) | copy-start | bytes 196612
  97.0 19.0 %all-to-all-start.2 = ((bf16[32,64,128]{2,1,0:T(8,128)(2,1)}), bf16[32,64,128]{2,1,0:T(8,128)(2,1)S(1)}, u32[]{:S(2)}, u32[]{:S(2)}) async-start(bf16[32,64,128]{2,1,0:T(8,128)(2,1)} %fusion.12), calls=%async_computation.2 | async-start | bytes 1048576 | tf_op jit(solution)/shard_map/all_to_all | solution.py:21
  117.0 39.9 %all-to-all-start.3 = ((bf16[32,320,128]{2,1,0:T(8,128)(2,1)}), bf16[32,320,128]{2,1,0:T(8,128)(2,1)}, u32[]{:S(2)}, u32[]{:S(2)}) async-start(bf16[32,320,128]{2,1,0:T(8,128)(2,1)} %broadcast_dynamic-update-slice_fusion), calls=%async_computation.3 | async-start | bytes 5242880 | tf_op jit(solution)/shard_map/all_to_all | solution.py:120
Sparse Core Ops, SparseCore 0:
  11.7 50.9 all-gather.1
where the time goes:
time: 170 us; the launch traced here: 169 us
  waiting for transfers between devices  74.3 us (44%)
  starting transfers between devices  26.1 us (15%)
  local copies, waits for them, and re-layouts  23.7 us (14%)
  matrix products  16.7 us (10%)
  between operations  14.9 us (9%)
  other arithmetic  12.7 us (7%)
    all_gather x1, waiting for transfers between devices, per_device(): lax.all_gather(packed, 'col', axis=0, tiled=True)  39.9 us
    all_to_all x1, waiting for transfers between devices, per_device(): incoming = lax.all_to_all(outgoing, 'row', 0, 0, tiled=True)  32.4 us
    all_to_all x2, starting transfers between devices, gather_rows(): got = lax.all_to_all(spread, axis_name, 0, 0, tiled=True)  12.8 us
    all_to_all x1, starting transfers between devices, reduce_rows(): got = lax.all_to_all(pieces, axis_name, 0, 0, tiled=True)  7.37 us
    reshape x1, local copies, waits for them, and re-layouts, per_device(): dense_t = jnp.transpose(dense, (0, 2, 4, 1, 3)).reshape(nodes, node_rows)  7.29 us
    all_to_all x1, starting transfers between devices, per_device(): incoming = lax.all_to_all(outgoing, 'row', 0, 0, tiled=True)  5.89 us
    dot_general x1, matrix products, per_device(): jnp.dot(dense_t, aggregated_grad, preferred_element_type=jnp.float32)  5.33 us
    broadcast_in_dim x2, local copies, waits for them, and re-layouts, gather_rows(): spread = jnp.broadcast_to(block[None], (parts,) + block.shape)  3.48 us
  transfers between devices with their start and end apart: 5, of which 4 were waited for; matrix products, arithmetic and copies ran while one was open for 19% of the time, Pallas kernels for 0%

commit v1 on v0

--- a/solution.py
+++ b/solution.py
@@ -3,6 +3,27 @@
 import jax.numpy as jnp
 from jax import lax
 from jax.sharding import PartitionSpec as P
+
+
+def gather_around(shard, axis, dim):
+    size, position, rows = (lax.axis_size(axis), lax.axis_index(axis), shard.shape[dim])
+    right = [(i, (i + 1) % size) for i in range(size)]
+    left = [(i, (i - 1) % size) for i in range(size)]
+    whole = jnp.zeros((*shard.shape[:dim], size * rows, *shard.shape[dim + 1 :]), shard.dtype)
+    whole = lax.dynamic_update_slice_in_dim(whole, shard, position * rows, axis=dim)
+    from_left = from_right = shard
+    half = size // 2
+    for hop in range(1, half + 1):
+        from_left = lax.ppermute(from_left, axis, right)
+        whole = lax.dynamic_update_slice_in_dim(
+            whole, from_left, (position - hop) % size * rows, axis=dim
+        )
+        if hop < size - half:
+            from_right = lax.ppermute(from_right, axis, left)
+            whole = lax.dynamic_update_slice_in_dim(
+                whole, from_right, (position + hop) % size * rows, axis=dim
+            )
+    return whole
 
 
 def silu_grad(preact):
@@ -36,9 +57,7 @@
         pos_row, positions[0, 0].astype(values.dtype).reshape(1, slots), (0, 0)
     )
     packed = jnp.concatenate([own_vals, pos_row, features, grad_out], axis=0)
-    all_packed = lax.all_gather(packed, "col", axis=0, tiled=True).reshape(
-        col_count, packed.shape[0], block_edge
-    )
+    all_packed = gather_around(packed, "col", 0).reshape(col_count, packed.shape[0], block_edge)
     tile_vals = all_packed.reshape(col_count, -1, block_edge, block_edge)[:, :slots]
     tile_pos = all_packed[:, slots * block_edge, :slots].astype(jnp.int32)
     cb = row_count * node_rows // col_count // block_edge

time: 170 us -> 162 us (0.953)
  waiting for transfers between devices: 74.3 us -> 57 us
  starting transfers between devices: 26.1 us -> 42.1 us
  between operations: 14.9 us -> 1.8 us
  local copies, waits for them, and re-layouts: 23.7 us -> 30.4 us
    all_gather x1 -> x0, waiting for transfers between devices: 39.9 us -> none  [per_device(): lax.all_gather(packed, 'col', axis=0, tiled=True)]
    ppermute x0 -> x7, waiting for transfers between devices: none -> 23.1 us  [the longest x4 23 us: gather_around(): from_left = lax.ppermute(from_left, axis, right)]
    ppermute x0 -> x7, starting transfers between devices: none -> 11.8 us  [the longest x3 9.27 us: gather_around(): from_right = lax.ppermute(from_right, axis, left)]
    dynamic_update_slice x0 -> x7, local copies, waits for them, and re-layouts: none -> 5.56 us  [the longest x4 3.19 us: gather_around(): lax.dynamic_update_slice_in_dim(whole, from_left, (position - hop) % size...]
    all_to_all x1, starting transfers between devices: 7.37 us -> 9.93 us  [reduce_rows(): got = lax.all_to_all(pieces, axis_name, 0, 0, tiled=True)]
    broadcast_in_dim x0 -> x1, local copies, waits for them, and re-layouts: none -> 1.93 us  [gather_around(): jnp.zeros((*shard.shape[:dim], size * rows, *shard.shape[dim + 1:]), shar...]
    all_to_all x2, starting transfers between devices: 12.8 us -> 14.5 us  [gather_rows(): got = lax.all_to_all(spread, axis_name, 0, 0, tiled=True)]
  transfers between devices with their start and end apart: 5 -> 11, of which waited for: 4 -> 5; matrix products, arithmetic and copies ran while one was open for 19% -> 23% of each run, Pallas kernels for 0% -> 0%
where the time goes in v1:
time: 162 us; the launch traced here: 161 us
  waiting for transfers between devices  57 us (35%)
  starting transfers between devices  42.1 us (26%)
  local copies, waits for them, and re-layouts  30.4 us (19%)
  matrix products  18.2 us (11%)
  other arithmetic  11.9 us (7%)
  between operations  1.8 us (1%)
    all_to_all x1, waiting for transfers between devices, per_device(): incoming = lax.all_to_all(outgoing, 'row', 0, 0, tiled=True)  32.4 us
    ppermute x4, waiting for transfers between devices, gather_around(): from_left = lax.ppermute(from_left, axis, right)  23 us
    all_to_all x2, starting transfers between devices, gather_rows(): got = lax.all_to_all(spread, axis_name, 0, 0, tiled=True)  14.5 us
    all_to_all x1, starting transfers between devices, reduce_rows(): got = lax.all_to_all(pieces, axis_name, 0, 0, tiled=True)  9.93 us
    ppermute x3, starting transfers between devices, gather_around(): from_right = lax.ppermute(from_right, axis, left)  9.27 us
    reshape x1, local copies, waits for them, and re-layouts, per_device(): dense_t = jnp.transpose(dense, (0, 2, 4, 1, 3)).reshape(nodes, node_rows)  7.31 us
    all_to_all x1, starting transfers between devices, per_device(): incoming = lax.all_to_all(outgoing, 'row', 0, 0, tiled=True)  5.89 us
    dot_general x1, matrix products, per_device(): jnp.dot(dense_t, aggregated_grad, preferred_element_type=jnp.float32)  5.33 us
  transfers between devices with their start and end apart: 11, of which 5 were waited for; matrix products, arithmetic and copies ran while one was open for 23% of the time, Pallas kernels for 0%

profile of v1, /device:TPU:1, one launch (start us, length us, event | category | flops | bytes accessed | tf_op | source)
XLA Modules:
  0.0 161.4 jit_solution(11887873867900331988)
XLA Ops:
  3.4 1.9 %broadcast_in_dim.8 = bf16[13312,128]{1,0:T(8,128)(2,1)} broadcast(bf16[]{:T(256)} %constant.78.clone.1), dimensions={} | broadcast | bytes 3407874 | tf_op jit(solution)/shard_map/broadcast_in_dim | solution.py:12
  6.3 2.5 %collective-permute-start = (bf16[1664,128]{1,0:T(8,128)(2,1)}, bf16[1664,128]{1,0:T(8,128)(2,1)S(1)}, u32[]{:S(2)}, u32[]{:S(2)}) collective-permute-start(bf16[1664,128]{1,0:T(8,128)(2,1)} %get-tuple-element.16), channel_id=1, source_target_pairs={{0,1},{1,2},{2,3},{3,4},{4,5},{5,6},{6,7},{7,0},{8,9},{9,10},{10,1... | collective-permute-start | bytes 1277960 | tf_op jit(solution)/shard_map/ppermute | solution.py:17
  8.7 3.9 %collective-permute-start.1 = (bf16[1664,128]{1,0:T(8,128)(2,1)}, bf16[1664,128]{1,0:T(8,128)(2,1)S(1)}, u32[]{:S(2)}, u32[]{:S(2)}) collective-permute-start(bf16[1664,128]{1,0:T(8,128)(2,1)} %get-tuple-element.16), channel_id=1, source_target_pairs={{0,7},{1,0},{2,1},{3,2},{4,3},{5,4},{6,5},{7,6},{8,15},{9,8},{10,9... | collective-permute-start | bytes 1277960 | tf_op jit(solution)/shard_map/ppermute | solution.py:22
  14.5 8.1 %all-to-all-start = ((bf16[32,256,128]{2,1,0:T(8,128)(2,1)}), bf16[32,256,128]{2,1,0:T(8,128)(2,1)}, u32[]{:S(2)}, u32[]{:S(2)}) async-start(bf16[32,256,128]{2,1,0:T(8,128)(2,1)} %broadcast_in_dim.9), calls=%async_computation | async-start | bytes 4194304 | tf_op jit(solution)/shard_map/all_to_all | solution.py:36
  22.8 2.7 %collective-permute-start.3 = (bf16[1664,128]{1,0:T(8,128)(2,1)S(1)}, bf16[1664,128]{1,0:T(8,128)(2,1)S(1)}, u32[]{:S(2)}, u32[]{:S(2)}) collective-permute-start(bf16[1664,128]{1,0:T(8,128)(2,1)S(1)} %collective-permute-done.1), channel_id=1, source_target_pairs={{0,7},{1,0},{2,1},{3,2},{4,3},{5,4},{6,5},{7,6},{8,15},{9,8},{10,9... | collective-permute-start | bytes 1277960 | tf_op jit(solution)/shard_map/ppermute | solution.py:22
  27.0 7.6 %collective-permute-done.2 = bf16[1664,128]{1,0:T(8,128)(2,1)S(1)} collective-permute-done((bf16[1664,128]{1,0:T(8,128)(2,1)S(1)}, bf16[1664,128]{1,0:T(8,128)(2,1)S(1)}, u32[]{:S(2)}, u32[]{:S(2)}) %collective-permute-start.2) | collective-permute-done | bytes 426016 | tf_op jit(solution)/shard_map/ppermute | solution.py:17
  34.6 2.7 %collective-permute-start.5 = (bf16[1664,128]{1,0:T(8,128)(2,1)S(1)}, bf16[1664,128]{1,0:T(8,128)(2,1)S(1)}, u32[]{:S(2)}, u32[]{:S(2)}) collective-permute-start(bf16[1664,128]{1,0:T(8,128)(2,1)S(1)} %collective-permute-done.3), channel_id=1, source_target_pairs={{0,7},{1,0},{2,1},{3,2},{4,3},{5,4},{6,5},{7,6},{8,15},{9,8},{10,9... | collective-permute-start | bytes 1277960 | tf_op jit(solution)/shard_map/ppermute | solution.py:22
  38.9 6.8 %collective-permute-done.4 = bf16[1664,128]{1,0:T(8,128)(2,1)S(1)} collective-permute-done((bf16[1664,128]{1,0:T(8,128)(2,1)S(1)}, bf16[1664,128]{1,0:T(8,128)(2,1)S(1)}, u32[]{:S(2)}, u32[]{:S(2)}) %collective-permute-start.4) | collective-permute-done | bytes 426016 | tf_op jit(solution)/shard_map/ppermute | solution.py:17
  47.3 8.6 %collective-permute-done.6 = bf16[1664,128]{1,0:T(8,128)(2,1)S(1)} collective-permute-done((bf16[1664,128]{1,0:T(8,128)(2,1)S(1)}, bf16[1664,128]{1,0:T(8,128)(2,1)S(1)}, u32[]{:S(2)}, u32[]{:S(2)}) %collective-permute-start.6) | collective-permute-done | bytes 426016 | tf_op jit(solution)/shard_map/ppermute | solution.py:17
  57.6 2.9 %fusion.5 = bf16[8,8,128,128]{3,1,2,0:T(8,128)(2,1)S(1)} fusion(bf16[8,8,128,128]{3,2,1,0:T(8,128)(2,1)} %bitcast.9, s32[8,8]{1,0:T(8,128)S(1)} %get-tuple-element.18), kind=kOutput, calls=%fused_computation.10 | convolution fusion | flops 17826304 | bytes 4194560 | tf_op jit(solution)/shard_map/tsc,tcjf->tsjf/dot_general | solution.py:80
  60.5 2.3 %fusion.1 = f32[8,8,128,128]{3,2,1,0:T(8,128)S(1)} fusion(bf16[8,13,128,128]{3,2,1,0:T(8,128)(2,1)} %bitcast.4, bf16[8,8,128,128]{3,1,2,0:T(8,128)(2,1)S(1)} %fusion.5), kind=kOutput, calls=%fused_computation.6 | convolution fusion | flops 268435456 | bytes 9699328 | tf_op jit(solution)/shard_map/tsij,tsjf->tsif/dot_general | solution.py:83
  64.5 6.4 %all-to-all-start.1 = ((bf16[8,256,128]{1,2,0:T(8,128)(2,1)}), bf16[8,256,128]{1,2,0:T(8,128)(2,1)}, u32[]{:S(2)}, u32[]{:S(2)}) async-start(bf16[8,256,128]{1,2,0:T(8,128)(2,1)} %broadcast_in_dim.10), calls=%async_computation.1 | async-start | bytes 1048576 | tf_op jit(solution)/shard_map/all_to_all | solution.py:36
  72.2 1.8 %slice.39 = bf16[8,8,128,128]{3,2,1,0:T(8,128)(2,1)S(1)} slice(bf16[8,13,128,128]{3,2,1,0:T(8,128)(2,1)} %bitcast.4), slice={[0:8], [0:8], [0:128], [0:128]} | slice | bytes 4194304 | tf_op jit(solution)/shard_map/slice | solution.py:61
  74.7 1.9 %convert_bitcast_fusion = bf16[8,2,8,128,128]{4,2,1,3,0:T(8,128)(2,1)S(1)} fusion(bf16[8,8,128,128]{3,2,1,0:T(8,128)(2,1)S(1)} %slice.39, s32[8,8]{1,0:T(8,128)S(1)} %bitcast.92), kind=kOutput, calls=%fused_computation.4 | convolution fusion | flops 35652608 | bytes 6291712 | tf_op jit(solution)/shard_map/tsp,tsij->tpij/dot_general | solution.py:68
  76.6 3.2 %copy.47 = bf16[8,2,8,128,128]{4,2,0,3,1:T(8,128)(2,1)} copy(bf16[8,2,8,128,128]{4,2,1,3,0:T(8,128)(2,1)S(1)} %convert_bitcast_fusion) | data formatting | bytes 8388608 | tf_op jit(solution)/shard_map/reshape | solution.py:71
  79.8 7.3 %reshape.122 = bf16[8192,256]{0,1:T(8,128)(2,1)} reshape(bf16[8,8,128,2,128]{2,1,0,4,3:T(8,128)(2,1)} %bitcast.83) | data formatting | bytes 8388608 | tf_op jit(solution)/shard_map/reshape | solution.py:88
  88.4 1.9 %fusion.34 = f32[256,1024]{1,0:T(8,128)S(1)} fusion(bf16[256,1024]{0,1:T(8,128)(2,1)} %bitcast.16, bf16[1024,1024]{1,0:T(8,128)(2,1)S(1)} %copy-done), kind=kOutput, calls=%fused_computation.70 | convolution fusion | flops 536870912 | bytes 3670016 | tf_op jit(solution)/shard_map/dot_general | solution.py:97
  90.6 2.1 %fusion.8 = (bf16[256,1024]{1,0:T(8,128)(2,1)S(1)}, f32[256,1024]{1,0:T(8,128)}) fusion(f32[32,8,8,128]{3,2,1,0:T(8,128)S(1)} %bitcast.87, f32[256,1024]{1,0:T(8,128)S(1)} %fusion.34, bf16[1024,1024]{1,0:T(8,128)(2,1)S(1)} %copy-done.5, bf16[32,8,8,128]{3,2,1,0:T(8,128)(2,1)S(1)} %bitcast.90), kind=kOutput, calls=%fused_computation.17 | convolution fusion | flops 539492352 | bytes 6291456 | tf_op jit(solution)/shard_map/dot_general | solution.py:97
  94.2 9.9 %all-to-all-start.2 = ((bf16[32,64,128]{2,1,0:T(8,128)(2,1)}), bf16[32,64,128]{2,1,0:T(8,128)(2,1)S(1)}, u32[]{:S(2)}, u32[]{:S(2)}) async-start(bf16[32,64,128]{2,1,0:T(8,128)(2,1)} %fusion.12), calls=%async_computation.2 | async-start | bytes 1048576 | tf_op jit(solution)/shard_map/all_to_all | solution.py:42
  104.1 5.3 %convolution_convert_fusion = bf16[8192,128]{1,0:T(8,128)(2,1)} fusion(bf16[8192,256]{0,1:T(8,128)(2,1)} %reshape.122, bf16[256,1024]{1,0:T(8,128)(2,1)S(1)} %get-tuple-element.20, bf16[1024,1024]{1,0:T(8,128)(2,1)S(1)} %copy-done, s32[]{:T(128)S(6)} %select_n.96), kind=kOutput, calls=%fused_computation | convolution fusion | flops 605061120 | bytes 7077892 | tf_op jit(solution)/shard_map/dot_general | solution.py:131
  109.4 3.5 %concatenate.10 = bf16[32,320,128]{2,1,0:T(8,128)(2,1)} pad(bf16[32,256,128]{2,1,0:T(8,128)(2,1)} %bitcast.84, bf16[]{:T(256)} %constant.78.clone.1), padding=0_0x0_64x0_0 | pad | bytes 4718594 | tf_op jit(solution)/shard_map/concatenate | solution.py:134
  116.8 5.9 %all-to-all-start.3 = ((bf16[32,320,128]{2,1,0:T(8,128)(2,1)}), bf16[32,320,128]{2,1,0:T(8,128)(2,1)}, u32[]{:S(2)}, u32[]{:S(2)}) async-start(bf16[32,320,128]{2,1,0:T(8,128)(2,1)} %broadcast_dynamic-update-slice_fusion), calls=%async_computation.3 | async-start | bytes 5242880 | tf_op jit(solution)/shard_map/all_to_all | solution.py:139
  124.2 32.4 %all-to-all-done.3 = bf16[32,320,128]{2,1,0:T(8,128)(2,1)} async-done(((bf16[32,320,128]{2,1,0:T(8,128)(2,1)}), bf16[32,320,128]{2,1,0:T(8,128)(2,1)}, u32[]{:S(2)}, u32[]{:S(2)}) %all-to-all-start.3) | async-done | bytes 2621472 | tf_op jit(solution)/shard_map/all_to_all | solution.py:139
  158.9 1.9 %convert_reduce_fusion = f32[256,128]{1,0:T(8,128)S(1)} fusion(bf16[32,320,128]{2,1,0:T(8,128)(2,1)} %all-to-all-done.3), kind=kLoop, calls=%fused_computation.3 | loop fusion | flops 2064384 | bytes 2228224 | tf_op jit(solution)/shard_map/reduce_sum | solution.py:140
  (54 shorter events, 26.1 us)
Async XLA Ops:
  0.6 87.8 %copy-start = (bf16[1024,1024]{1,0:T(8,128)(2,1)S(1)}, bf16[1024,1024]{1,0:T(8,128)(2,1)}, u32[]{:S(2)}) copy-start(bf16[1024,1024]{1,0:T(8,128)(2,1)} %param.9) | copy-start | bytes 6291460
  0.6 4.7 %copy-start.2 = (bf16[256,128]{1,0:T(8,128)(2,1)S(1)}, bf16[256,128]{1,0:T(8,128)(2,1)}, u32[]{:S(2)}) copy-start(bf16[256,128]{1,0:T(8,128)(2,1)} %param.7) | copy-start | bytes 196612
  0.7 4.6 %copy-start.4 = (bf16[256,128]{1,0:T(8,128)(2,1)S(1)}, bf16[256,128]{1,0:T(8,128)(2,1)}, u32[]{:S(2)}) copy-start(bf16[256,128]{1,0:T(8,128)(2,1)} %param.8) | copy-start | bytes 196612
  6.3 16.4 %collective-permute-start = (bf16[1664,128]{1,0:T(8,128)(2,1)}, bf16[1664,128]{1,0:T(8,128)(2,1)S(1)}, u32[]{:S(2)}, u32[]{:S(2)}) collective-permute-start(bf16[1664,128]{1,0:T(8,128)(2,1)} %get-tuple-element.16), channel_id=1, source_target_pairs={{0,1},{1,2},{2,3},{3,4},{4,5},{5,6},{6,7},{7,0},{8,9},{9,10},{10,1... | collective-permute-start | bytes 1277960 | tf_op jit(solution)/shard_map/ppermute | solution.py:17
  8.7 14.1 %collective-permute-start.1 = (bf16[1664,128]{1,0:T(8,128)(2,1)}, bf16[1664,128]{1,0:T(8,128)(2,1)S(1)}, u32[]{:S(2)}, u32[]{:S(2)}) collective-permute-start(bf16[1664,128]{1,0:T(8,128)(2,1)} %get-tuple-element.16), channel_id=1, source_target_pairs={{0,7},{1,0},{2,1},{3,2},{4,3},{5,4},{6,5},{7,6},{8,15},{9,8},{10,9... | collective-permute-start | bytes 1277960 | tf_op jit(solution)/shard_map/ppermute | solution.py:22
  14.5 43.1 %all-to-all-start = ((bf16[32,256,128]{2,1,0:T(8,128)(2,1)}), bf16[32,256,128]{2,1,0:T(8,128)(2,1)}, u32[]{:S(2)}, u32[]{:S(2)}) async-start(bf16[32,256,128]{2,1,0:T(8,128)(2,1)} %broadcast_in_dim.9), calls=%async_computation | async-start | bytes 4194304 | tf_op jit(solution)/shard_map/all_to_all | solution.py:36
  22.7 11.9 %collective-permute-start.2 = (bf16[1664,128]{1,0:T(8,128)(2,1)S(1)}, bf16[1664,128]{1,0:T(8,128)(2,1)S(1)}, u32[]{:S(2)}, u32[]{:S(2)}) collective-permute-start(bf16[1664,128]{1,0:T(8,128)(2,1)S(1)} %collective-permute-done), channel_id=1, source_target_pairs={{0,1},{1,2},{2,3},{3,4},{4,5},{5,6},{6,7},{7,0},{8,9},{9,10},{10,1... | collective-permute-start | bytes 1277960 | tf_op jit(solution)/shard_map/ppermute | solution.py:17
  22.8 11.8 %collective-permute-start.3 = (bf16[1664,128]{1,0:T(8,128)(2,1)S(1)}, bf16[1664,128]{1,0:T(8,128)(2,1)S(1)}, u32[]{:S(2)}, u32[]{:S(2)}) collective-permute-start(bf16[1664,128]{1,0:T(8,128)(2,1)S(1)} %collective-permute-done.1), channel_id=1, source_target_pairs={{0,7},{1,0},{2,1},{3,2},{4,3},{5,4},{6,5},{7,6},{8,15},{9,8},{10,9... | collective-permute-start | bytes 1277960 | tf_op jit(solution)/shard_map/ppermute | solution.py:22
  34.6 11.1 %collective-permute-start.4 = (bf16[1664,128]{1,0:T(8,128)(2,1)S(1)}, bf16[1664,128]{1,0:T(8,128)(2,1)S(1)}, u32[]{:S(2)}, u32[]{:S(2)}) collective-permute-start(bf16[1664,128]{1,0:T(8,128)(2,1)S(1)} %collective-permute-done.2), channel_id=1, source_target_pairs={{0,1},{1,2},{2,3},{3,4},{4,5},{5,6},{6,7},{7,0},{8,9},{9,10},{10,1... | collective-permute-start | bytes 1277960 | tf_op jit(solution)/shard_map/ppermute | solution.py:17
  34.6 11.9 %collective-permute-start.5 = (bf16[1664,128]{1,0:T(8,128)(2,1)S(1)}, bf16[1664,128]{1,0:T(8,128)(2,1)S(1)}, u32[]{:S(2)}, u32[]{:S(2)}) collective-permute-start(bf16[1664,128]{1,0:T(8,128)(2,1)S(1)} %collective-permute-done.3), channel_id=1, source_target_pairs={{0,7},{1,0},{2,1},{3,2},{4,3},{5,4},{6,5},{7,6},{8,15},{9,8},{10,9... | collective-permute-start | bytes 1277960 | tf_op jit(solution)/shard_map/ppermute | solution.py:22
  45.7 10.2 %collective-permute-start.6 = (bf16[1664,128]{1,0:T(8,128)(2,1)S(1)}, bf16[1664,128]{1,0:T(8,128)(2,1)S(1)}, u32[]{:S(2)}, u32[]{:S(2)}) collective-permute-start(bf16[1664,128]{1,0:T(8,128)(2,1)S(1)} %collective-permute-done.4), channel_id=1, source_target_pairs={{0,1},{1,2},{2,3},{3,4},{4,5},{5,6},{6,7},{7,0},{8,9},{9,10},{10,1... | collective-permute-start | bytes 1277960 | tf_op jit(solution)/shard_map/ppermute | solution.py:17
  64.5 23.9 %all-to-all-start.1 = ((bf16[8,256,128]{1,2,0:T(8,128)(2,1)}), bf16[8,256,128]{1,2,0:T(8,128)(2,1)}, u32[]{:S(2)}, u32[]{:S(2)}) async-start(bf16[8,256,128]{1,2,0:T(8,128)(2,1)} %broadcast_in_dim.10), calls=%async_computation.1 | async-start | bytes 1048576 | tf_op jit(solution)/shard_map/all_to_all | solution.py:36
  88.4 2.0 %copy-start.3 = (bf16[1,256,8,128]{3,2,1,0:T(8,128)(2,1)S(1)}, bf16[1,256,8,128]{3,2,1,0:T(8,128)(2,1)}, u32[]{:S(2)}) copy-start(bf16[1,256,8,128]{3,2,1,0:T(8,128)(2,1)} %get-tuple-element.15) | copy-start | bytes 1572868
  88.4 2.0 %copy-start.1 = (f32[1,256,8,128]{3,2,1,0:T(8,128)S(1)}, f32[1,256,8,128]{3,2,1,0:T(8,128)}, u32[]{:S(2)}) copy-start(f32[1,256,8,128]{3,2,1,0:T(8,128)} %get-tuple-element.14) | copy-start | bytes 3145732
  88.4 2.2 %copy-start.5 = (bf16[1024,1024]{1,0:T(8,128)(2,1)S(1)}, bf16[1024,1024]{1,0:T(8,128)(2,1)}, u32[]{:S(2)}) copy-start(bf16[1024,1024]{1,0:T(8,128)(2,1)} %param.10) | copy-start | bytes 6291460
  94.2 21.5 %all-to-all-start.2 = ((bf16[32,64,128]{2,1,0:T(8,128)(2,1)}), bf16[32,64,128]{2,1,0:T(8,128)(2,1)S(1)}, u32[]{:S(2)}, u32[]{:S(2)}) async-start(bf16[32,64,128]{2,1,0:T(8,128)(2,1)} %fusion.12), calls=%async_computation.2 | async-start | bytes 1048576 | tf_op jit(solution)/shard_map/all_to_all | solution.py:42
  116.8 39.9 %all-to-all-start.3 = ((bf16[32,320,128]{2,1,0:T(8,128)(2,1)}), bf16[32,320,128]{2,1,0:T(8,128)(2,1)}, u32[]{:S(2)}, u32[]{:S(2)}) async-start(bf16[32,320,128]{2,1,0:T(8,128)(2,1)} %broadcast_dynamic-update-slice_fusion), calls=%async_computation.3 | async-start | bytes 5242880 | tf_op jit(solution)/shard_map/all_to_all | solution.py:139
